TPU v7x, 32 devices: a whole 2x2x4 slice. The times are simulated.
32 devices in a mesh: tile: 8 (over y, x, core), dir: 4 (over z).
Axes of the slice: x: 2, y: 2, z: 4, core: 2. Of those that a mesh axis runs over, the one named last changes fastest.
Arguments:
- screens: bfloat16 [6, 512, 2048], P(None, 'tile'), may hold values from -13 to 13
- ray_shift: int32 [16, 6, 2], P('dir'), may hold values from -128 to 2047, as said below
- ray_weight: float32 [16, 6, 4], P('dir'), may hold values from 0 to 0.5
- influence_index: int32 [512, 16, 16], P('tile', 'dir'), may hold values from 0 to 69, as said below
- influence: bfloat16 [512, 16, 16, 128], P('tile', 'dir'), may hold values from 0 to 0.22
- pupil_mask: int32 [512, 2048], P('tile', 'dir'), may hold values 0 or 1
- petal: int32 [24, 48], P('tile', 'dir'), may hold values from 0 to 6
Outputs:
- commands: float32 [24, 48], P('tile', 'dir')
- corrected: bfloat16 [16, 512, 2048], P('dir', 'tile')
Inputs may be any that keep to these rules, and one draw needn't show every extreme that they name: ray_shift[..., 0], the row offset, lies in -128 to 127 and reaches both ends; ray_shift[..., 1], the column offset, lies in 0 to 2047. `influence_index`: each entry names a grid point of the tile's own actuator block extended by one actuator on each side, flattened row by row with 14 points a row; entries may repeat.
All inputs are finite; a program needn't handle non-finite values. No bound on the sum of `pupil_mask` on one device may be relied on, other than what follows from the above.
Results may differ from a plain program's by a relative error of at most 0.007.
Values may be sent and summed in bfloat16 or wider, within the bound.
No kernel may reach another device: no remote copies, remote signals or barrier semaphores. Data moves between devices by JAX's collectives and lax.ppermute only.
A program may use at most 128 MiB of HBM per device.

v0:
```python
import jax
import jax.numpy as jnp
from jax import lax
from jax.sharding import PartitionSpec as P

SPAN = 2
AR_DEV = 3
AC_DEV = 12
ITERS = 3


ridge_weight = 1.0
piston_weight = 0.002
highest = lax.Precision.HIGHEST


def passed_along(array, axis, by):
    size = lax.axis_size(axis)
    return lax.ppermute(array, axis, [(i, (i + by) % size) for i in range(size)])


def padded_2(array, sides, width):
    for axis, dim in sides:
        size, length = (lax.axis_size(axis), array.shape[dim])
        up = [(i, (i + 1) % size) for i in range(size - 1)]
        down = [(j, i) for i, j in up]
        last = lax.slice_in_dim(array, length - width, length, axis=dim)
        first = lax.slice_in_dim(array, 0, width, axis=dim)
        before = lax.ppermute(last, axis, up)
        after = lax.ppermute(first, axis, down)
        array = jnp.concatenate([before, array, after], axis=dim)
    return array


def band_stack_whole(piece):
    bands = []
    for offset in range(SPAN, -SPAN - 1, -1):
        if offset == 0:
            bands.append(piece)
        else:
            bands.append(passed_along(piece, "tile", offset))
    return jnp.concatenate(bands, axis=1)


def trace_rows(padded_rim, shifts, layer_gains, rim_depth, band_rows):
    summed = jnp.zeros((band_rows, padded_rim.shape[2]), jnp.float32)
    for layer_index in range(padded_rim.shape[0]):
        window = lax.dynamic_slice_in_dim(
            padded_rim[layer_index], rim_depth + shifts[layer_index, 0], band_rows + 1, 0
        ).astype(jnp.float32)
        window = jnp.roll(window, -shifts[layer_index, 1], axis=1)
        beside = jnp.roll(window, -1, axis=1)
        gains = layer_gains[layer_index]
        summed = summed + (
            gains[0] * window[:-1]
            + gains[1] * beside[:-1]
            + gains[2] * window[1:]
            + gains[3] * beside[1:]
        )
    return summed


def fold_rims(gathered):
    padded = padded_2(gathered, (("tile", 0), ("dir", 1)), 1)
    grid_rows = gathered.shape[0] - 2
    grid_columns = gathered.shape[1] - 2
    interior = gathered[1:-1, 1:-1]
    interior = interior.at[:, 0].add(padded[2 : grid_rows + 2, 0])
    interior = interior.at[:, -1].add(padded[2 : grid_rows + 2, -1])
    interior = interior.at[0, :].add(padded[0, 2 : grid_columns + 2])
    interior = interior.at[-1, :].add(padded[-1, 2 : grid_columns + 2])
    interior = interior.at[0, 0].add(padded[0, 0])
    interior = interior.at[0, -1].add(padded[0, -1])
    interior = interior.at[-1, 0].add(padded[-1, 0])
    interior = interior.at[-1, -1].add(padded[-1, -1])
    return interior


def on_device(screens, ray_shift, ray_weight, influence_index, influence, pupil_mask, petal):
    band_rows = screens.shape[1]
    rim_depth = SPAN * band_rows
    padded_rim = band_stack_whole(screens)
    phases = [
        trace_rows(padded_rim, ray_shift[member], ray_weight[member], rim_depth, band_rows)
        for member in range(ray_shift.shape[0])
    ]
    direction_count = ray_shift.shape[0] * lax.axis_size("dir")
    summed = phases[0]
    for member in range(1, len(phases)):
        summed = summed + phases[member]
    mean_phase = (
        lax.psum_scatter(
            summed.astype(jnp.bfloat16), "dir", scatter_dimension=1, tiled=True
        ).astype(jnp.float32)
        / direction_count
    )
    tiles_here = influence.shape[1]
    near_count = influence.shape[2]
    values = influence.astype(jnp.float32)
    extent = (AR_DEV + 2) * (AC_DEV + 2)
    selector = (
        influence_index.reshape(-1)[:, None] == jnp.arange(extent, dtype=jnp.int32)[None, :]
    ).astype(jnp.float32)
    weights = pupil_mask.astype(jnp.float32)
    active = (petal < 6).astype(jnp.float32)
    petals = (petal.reshape(-1)[:, None] == jnp.arange(6, dtype=jnp.int32)[None, :]).astype(
        jnp.float32
    )

    def surface(commands):
        extended = padded_2(commands, (("tile", 0), ("dir", 1)), 1)
        picked = jnp.dot(selector, extended.reshape(-1), precision=highest).reshape(
            band_rows, tiles_here, near_count
        )
        tile_sums = jnp.einsum("rckp,rck->rcp", values, picked, precision=highest)
        return tile_sums.reshape(band_rows, tiles_here * 128)

    def spread(field):
        tile_terms = jnp.einsum(
            "rckp,rcp->rck", values, field.reshape(band_rows, tiles_here, 128), precision=highest
        )
        gathered = jnp.dot(tile_terms.reshape(-1), selector, precision=highest).reshape(
            AR_DEV + 2, AC_DEV + 2
        )
        return fold_rims(gathered)

    def global_norm(residual):
        return lax.psum(jnp.sum(residual * residual), ("tile", "dir"))

    rhs = active * spread(weights * mean_phase)
    commands = jnp.zeros_like(rhs)
    residual = rhs
    direction = rhs
    norm_now = global_norm(residual)
    for step_index in range(ITERS):
        local_part = active * spread(weights * surface(direction)) + ridge_weight * direction
        local_totals = jnp.dot(direction.reshape(-1), petals, precision=highest)
        petal_totals, partial_dot = lax.psum(
            (local_totals, jnp.sum(direction * local_part)), ("tile", "dir")
        )
        applied = local_part + piston_weight * jnp.dot(
            petals, petal_totals, precision=highest
        ).reshape(direction.shape)
        curvature = partial_dot + piston_weight * jnp.sum(petal_totals * petal_totals)
        step_size = norm_now / curvature
        commands = commands + step_size * direction
        residual = residual - step_size * applied
        norm_next = global_norm(residual)
        direction = residual + norm_next / norm_now * direction
        norm_now = norm_next
    fitted = surface(commands)
    whole_band = lax.all_gather(fitted.astype(jnp.bfloat16), "dir", axis=1, tiled=True).astype(
        fitted.dtype
    )
    corrected = jnp.stack([(phase_rows - whole_band).astype(jnp.bfloat16) for phase_rows in phases])
    return (commands, corrected)


def solution(mesh):
    in_specs = (
        P(None, "tile", None),
        P("dir", None, None),
        P("dir", None, None),
        P("tile", "dir", None),
        P("tile", "dir", None, None),
        P("tile", "dir"),
        P("tile", "dir"),
    )
    out_specs = (P("tile", "dir"), P("dir", "tile", None))
    return jax.shard_map(
        on_device, mesh=mesh, in_specs=in_specs, out_specs=out_specs, check_vma=False
    )
```

profile of v0, /device:TPU:0, one launch (start us, length us, event | category | flops | bytes accessed | tf_op | source)
XLA Modules:
  0.0 727.4 jit_solution(10193905271201965904)
XLA Ops:
  7.2 3.0 collective-permute-start
  10.2 2.6 collective-permute-start.2
  71.6 7.1 collective-permute-done.1
  82.0 31.5 %collective-permute-done.3 = bf16[6,64,2048]{2,1,0:T(8,128)(2,1)S(1)} collective-permute-done((bf16[6,64,2048]{2,1,0:T(8,128)(2,1)}, bf16[6,64,2048]{2,1,0:T(8,128)(2,1)S(1)}, u32[]{:S(2)}, u32[]{:S(2)}) %collective-permute-start.3) | collective-permute-done | bytes 1572896 | tf_op jit(solution)/shard_map/ppermute | solution.py:19
  164.8 96.7 %add_convert_fusion = (bf16[64,2048]{1,0:T(8,128)(2,1)}, f32[64,2048]{1,0:T(8,128)}, f32[64,2048]{1,0:T(8,128)}, f32[64,2048]{1,0:T(8,128)}, f32[64,2048]{1,0:T(8,128)}) fusion(f32[65,1]{1,0:T(8,128)} %slice.2466, f32[65,2047]{1,0:T(8,128)} %slice.2465, f32[]{:T(128)} %bitcast.97, f32[65,2048]{1,0:T(8,128)} %copy-done.28, f32[]{:T(128)} %bitcast.96, ...), kind=kLoop, calls=%fused_computation.395 | loop fusion | flops 31457280 | bytes 40305024 | tf_op jit(solution)/shard_map/convert_element_type | solution.py:93
  265.2 16.4 %reduce-scatter.2.cloned.1.call-done = bf16[64,512]{1,0:T(8,128)(2,1)} async-done(((bf16[64,2048]{1,0:T(8,128)(2,1)}), bf16[64,512]{1,0:T(8,128)(2,1)}) %reduce-scatter.2.cloned.1.call-update) | async-done | bytes 65552 | tf_op jit(solution)/shard_map/reduce_scatter | solution.py:92
  288.3 3.5 collective-permute-done.5
  295.2 3.4 collective-permute-done.7
  301.5 1.8 dynamic-slice.243
  311.9 3.1 collective-permute-start.8
  316.5 2.2 collective-permute-done.9
  318.8 3.7 collective-permute-start.10
  323.8 4.2 collective-permute-done.11
  328.2 2.5 fusion.21
  334.9 2.8 collective-permute-start.12
  339.1 2.7 collective-permute-done.13
  342.0 2.3 collective-permute-start.14
  346.4 3.4 collective-permute-done.15
  352.7 1.8 dynamic-slice.244
  363.5 41.3 %all-reduce.2 = (f32[6]{0:T(128)S(1)}, f32[]{:T(128)}, f32[]{:T(128)}) all-reduce(f32[6]{0:T(128)S(1)} %convolution_bitcast_fusion.4, f32[]{:T(128)} %get-tuple-element.388, f32[]{:T(128)} %get-tuple-element.387), channel_id=1, replica_groups=mesh['tile'=8,'dir'=4] {'tile','dir'}, use_global_device_ids=true, to_apply=%region_7.9 | all-reduce | flops 8 | bytes 64 | tf_op jit(solution)/shard_map/psum | solution.py:138
  408.4 42.2 %psum.66 = f32[]{:T(128)} all-reduce(f32[]{:T(128)} %get-tuple-element.398), channel_id=1, replica_groups=mesh['tile'=8,'dir'=4] {'tile','dir'}, use_global_device_ids=true, to_apply=%region_10.12 | all-reduce | flops 1 | bytes 8 | tf_op jit(solution)/shard_map/psum | solution.py:128
  454.9 4.0 collective-permute-done.17
  459.0 1.9 collective-permute-start.18
  462.2 4.2 collective-permute-done.19
  466.6 2.5 fusion.19
  470.3 1.7 fusion.270
  473.3 2.8 collective-permute-start.20
  477.5 2.6 collective-permute-done.21
  480.3 2.6 collective-permute-start.22
  484.9 3.4 collective-permute-done.23
  491.2 1.8 dynamic-slice.245
  501.9 42.4 %all-reduce.1 = (f32[6]{0:T(128)S(1)}, f32[]{:T(128)}) all-reduce(f32[6]{0:T(128)S(1)} %convolution_bitcast_fusion.2, f32[]{:T(128)} %multiply_reduce_fusion.1), channel_id=1, replica_groups=mesh['tile'=8,'dir'=4] {'tile','dir'}, use_global_device_ids=true, to_apply=%region_13.15 | all-reduce | flops 7 | bytes 56 | tf_op jit(solution)/shard_map/psum | solution.py:138
  547.8 40.2 %psum.69 = f32[]{:T(128)} all-reduce(f32[]{:T(128)} %get-tuple-element.396), channel_id=1, replica_groups=mesh['tile'=8,'dir'=4] {'tile','dir'}, use_global_device_ids=true, to_apply=%region_16.18 | all-reduce | flops 1 | bytes 8 | tf_op jit(solution)/shard_map/psum | solution.py:128
  592.3 4.0 collective-permute-done.25
  596.4 3.9 collective-permute-start.26
  601.9 3.9 collective-permute-done.27
  606.0 2.5 fusion.17
  612.7 2.8 collective-permute-start.28
  617.0 2.6 collective-permute-done.29
  619.7 2.6 collective-permute-start.30
  624.4 3.4 collective-permute-done.31
  630.7 1.8 dynamic-slice.246
  641.3 40.6 %all-reduce = (f32[]{:T(128)}, f32[6]{0:T(128)S(1)}) all-reduce(f32[]{:T(128)} %fusion.224, f32[6]{0:T(128)S(1)} %convolution_bitcast_fusion), channel_id=1, replica_groups=mesh['tile'=8,'dir'=4] {'tile','dir'}, use_global_device_ids=true, to_apply=%region_18.20 | all-reduce | flops 7 | bytes 56 | tf_op jit(solution)/shard_map/psum | solution.py:138
  687.2 4.2 collective-permute-done.33
  691.5 3.6 collective-permute-start.34
  696.4 4.2 collective-permute-done.35
  700.8 2.5 fusion.15
  704.5 14.4 %all_gather.3 = bf16[64,2048]{1,0:T(8,128)(2,1)S(1)} all-gather(bf16[64,512]{1,0:T(8,128)(2,1)S(1)} %bitcast.390), channel_id=1, replica_groups=mesh['tile'=8,'dir'=4] {'dir'}, dimensions={1}, use_global_device_ids=true | all-gather | bytes 327680 | tf_op jit(solution)/shard_map/all_gather | solution.py:152
  (392 shorter events, 145.0 us)
Async XLA Ops:
  7.2 275.4 %copy-start = (bf16[64,4,16,128]{3,2,1,0:T(8,128)(2,1)S(1)}, bf16[64,4,16,128]{3,2,1,0:T(8,128)(2,1)}, u32[]{:S(2)}) copy-start(bf16[64,4,16,128]{3,2,1,0:T(8,128)(2,1)} %param.77) | copy-start | bytes 3145732
  7.2 59.3 %copy-start.36 = (f32[4,6,4]{1,2,0:T(4,128)S(1)}, f32[4,6,4]{1,2,0:T(4,128)}, u32[]{:S(2)}) copy-start(f32[4,6,4]{1,2,0:T(4,128)} %param.75) | copy-start | bytes 1156
  7.2 58.0 %copy-start.39 = (s32[3,12]{1,0:T(4,128)S(1)}, s32[3,12]{1,0:T(4,128)}, u32[]{:S(2)}) copy-start(s32[3,12]{1,0:T(4,128)} %param.79) | copy-start | bytes 436
  7.2 274.3 %reduce-scatter.2.cloned.1.call-start = ((), (), s32[]{:S(2)}) async-start(), calls=%async_computation.1 | async-start | bytes 327680 | tf_op jit(solution)/shard_map/reduce_scatter | solution.py:92
  7.2 62.8 %collective-permute-start = (bf16[6,64,2048]{2,1,0:T(8,128)(2,1)}, bf16[6,64,2048]{2,1,0:T(8,128)(2,1)}, u32[]{:S(2)}, u32[]{:S(2)}) collective-permute-start(bf16[6,64,2048]{2,1,0:T(8,128)(2,1)} %param.73), channel_id=1, source_target_pairs={{0,8},{4,12},{8,16},{12,20},{16,24},{20,28},{24,0},{28,4},{1,9},{5... | collective-permute-start | bytes 4718600 | tf_op jit(solution)/shard_map/ppermute | solution.py:19
  10.2 68.5 %collective-permute-start.1 = (bf16[6,64,2048]{2,1,0:T(8,128)(2,1)}, bf16[6,64,2048]{2,1,0:T(8,128)(2,1)}, u32[]{:S(2)}, u32[]{:S(2)}) collective-permute-start(bf16[6,64,2048]{2,1,0:T(8,128)(2,1)} %param.73), channel_id=1, source_target_pairs={{0,4},{4,8},{8,12},{12,16},{16,20},{20,24},{24,28},{28,0},{1,5},{5... | collective-permute-start | bytes 4718600 | tf_op jit(solution)/shard_map/ppermute | solution.py:19
  10.2 70.2 %collective-permute-start.2 = (bf16[6,64,2048]{2,1,0:T(8,128)(2,1)}, bf16[6,64,2048]{2,1,0:T(8,128)(2,1)}, u32[]{:S(2)}, u32[]{:S(2)}) collective-permute-start(bf16[6,64,2048]{2,1,0:T(8,128)(2,1)} %param.73), channel_id=1, source_target_pairs={{0,28},{4,0},{8,4},{12,8},{16,12},{20,16},{24,20},{28,24},{1,29},{... | collective-permute-start | bytes 4718600 | tf_op jit(solution)/shard_map/ppermute | solution.py:19
  12.9 100.6 %collective-permute-start.3 = (bf16[6,64,2048]{2,1,0:T(8,128)(2,1)}, bf16[6,64,2048]{2,1,0:T(8,128)(2,1)S(1)}, u32[]{:S(2)}, u32[]{:S(2)}) collective-permute-start(bf16[6,64,2048]{2,1,0:T(8,128)(2,1)} %param.73), channel_id=1, source_target_pairs={{0,24},{4,28},{8,0},{12,4},{16,8},{20,12},{24,16},{28,20},{1,25},{... | collective-permute-start | bytes 4718600 | tf_op jit(solution)/shard_map/ppermute | solution.py:19
  263.4 21.1 %copy-start.38 = (s32[4096]{0:T(1024)S(1)}, s32[4096]{0:T(1024)}, u32[]{:S(2)}) copy-start(s32[4096]{0:T(1024)} %eq.69) | copy-start | bytes 49156
  282.5 29.2 %copy-start.40 = (s32[3,12]{1,0:T(4,128)S(1)}, s32[3,12]{1,0:T(4,128)}, u32[]{:S(2)}) copy-start(s32[3,12]{1,0:T(4,128)} %param.79) | copy-start | bytes 436
  282.5 33.7 %copy-start.41 = (s32[36]{0:T(128)S(1)}, s32[36]{0:T(128)}, u32[]{:S(2)}) copy-start(s32[36]{0:T(128)} %eq.77) | copy-start | bytes 436
  285.6 2.7 collective-permute-start.4
  286.9 4.8 collective-permute-start.5
  291.8 2.6 collective-permute-start.6
  293.1 5.5 collective-permute-start.7
  311.9 4.6 collective-permute-start.8
  315.0 3.7 collective-permute-start.9
  318.8 5.0 collective-permute-start.10
  322.5 5.5 collective-permute-start.11
  334.9 4.2 collective-permute-start.12
  337.8 4.1 collective-permute-start.13
  342.0 3.6 collective-permute-start.14
  344.3 5.5 collective-permute-start.15
  452.1 2.8 collective-permute-start.16
  453.4 5.5 collective-permute-start.17
  459.0 3.2 collective-permute-start.18
  460.9 5.5 collective-permute-start.19
  473.3 4.2 collective-permute-start.20
  476.2 4.0 collective-permute-start.21
  480.3 3.9 collective-permute-start.22
  482.8 5.5 collective-permute-start.23
  589.5 2.8 collective-permute-start.24
  590.8 5.5 collective-permute-start.25
  596.4 5.5 collective-permute-start.26
  600.3 5.5 collective-permute-start.27
  612.7 4.2 collective-permute-start.28
  615.6 4.0 collective-permute-start.29
  619.7 3.9 collective-permute-start.30
  622.3 5.5 collective-permute-start.31
  684.6 19.9 %copy-start.37 = (f32[3,12]{1,0:T(4,128)}, f32[3,12]{1,0:T(4,128)S(1)}, u32[]{:S(2)}) copy-start(f32[3,12]{1,0:T(4,128)S(1)} %multiply_add_fusion) | copy-start | bytes 436
  684.6 2.6 collective-permute-start.32
  685.9 5.5 collective-permute-start.33
  691.5 4.9 collective-permute-start.34
  695.1 5.5 collective-permute-start.35
  703.3 15.6 %copy-start.29 = (f32[64,2048]{1,0:T(8,128)S(1)}, f32[64,2048]{1,0:T(8,128)}, u32[]{:S(2)}) copy-start(f32[64,2048]{1,0:T(8,128)} %get-tuple-element.403) | copy-start | bytes 1572868
  703.3 15.6 %copy-start.30 = (f32[64,2048]{1,0:T(8,128)S(1)}, f32[64,2048]{1,0:T(8,128)}, u32[]{:S(2)}) copy-start(f32[64,2048]{1,0:T(8,128)} %get-tuple-element.404) | copy-start | bytes 1572868
  703.3 15.6 %copy-start.31 = (f32[64,2048]{1,0:T(8,128)S(1)}, f32[64,2048]{1,0:T(8,128)}, u32[]{:S(2)}) copy-start(f32[64,2048]{1,0:T(8,128)} %get-tuple-element.405) | copy-start | bytes 1572868
  703.4 15.6 %copy-start.32 = (f32[64,2048]{1,0:T(8,128)S(1)}, f32[64,2048]{1,0:T(8,128)}, u32[]{:S(2)}) copy-start(f32[64,2048]{1,0:T(8,128)} %get-tuple-element.406) | copy-start | bytes 1572868
  (35 other events, 105.4 us)
Sparse Core Ops, SparseCore 0:
  261.6 19.8 reduce-scatter.1
where the time goes:
time: 734 us; the launch traced here: 727 us
  blocking collectives  221 us (30%)
  other arithmetic  123 us (17%)
  waiting for transfers between devices  111 us (15%)
  between operations  96.2 us (13%)
  local copies, waits for them, and re-layouts  84.1 us (11%)
  starting transfers between devices  65.3 us (9%)
  matrix products  25.9 us (4%)
    psum x3, blocking collectives, on_device(): lax.psum((local_totals, jnp.sum(direction * local_part)), ('tile', 'dir'))  124 us
    convert_element_type x1, other arithmetic, on_device(): summed.astype(jnp.bfloat16)  96.7 us
    psum x2, blocking collectives, global_norm(): return lax.psum(jnp.sum(residual * residual), ('tile', 'dir'))  82.5 us
    ppermute x16, waiting for transfers between devices, padded_2(): after = lax.ppermute(first, axis, down)  56.1 us
    ppermute x16, starting transfers between devices, padded_2(): before = lax.ppermute(last, axis, up)  38.6 us
    ppermute x4, waiting for transfers between devices, passed_along(): lax.ppermute(array, axis, [(i, (i + by) % size) for i in range(size)])  38.6 us
    slice x52, local copies, waits for them, and re-layouts, trace_rows(): beside = jnp.roll(window, -1, axis=1)  37.7 us
    ppermute x16, starting transfers between devices, padded_2(): after = lax.ppermute(first, axis, down)  20.9 us
  transfers between devices with their start and end apart: 37, of which 19 were waited for; matrix products, arithmetic and copies ran while one was open for 3% of the time, Pallas kernels for 0%

commit v1 on v0

v1 whole, which is shorter than its diff:
```python
import jax
import jax.numpy as jnp
from jax import lax
from jax.sharding import PartitionSpec as P

SPAN = 2
AR_DEV = 3
AC_DEV = 12
ITERS = 3


ridge_weight = 1.0
piston_weight = 0.002
highest = lax.Precision.HIGHEST


def passed_along(array, axis, by):
    size = lax.axis_size(axis)
    return lax.ppermute(array, axis, [(i, (i + by) % size) for i in range(size)])


def band_stack_whole(piece):
    bands = []
    for offset in range(SPAN, -SPAN - 1, -1):
        if offset == 0:
            bands.append(piece)
        else:
            bands.append(passed_along(piece, "tile", offset))
    return jnp.concatenate(bands, axis=1)


def trace_rows(padded_rim, shifts, layer_gains, rim_depth, band_rows):
    summed = jnp.zeros((band_rows, padded_rim.shape[2]), jnp.float32)
    for layer_index in range(padded_rim.shape[0]):
        window = lax.dynamic_slice_in_dim(
            padded_rim[layer_index], rim_depth + shifts[layer_index, 0], band_rows + 1, 0
        ).astype(jnp.float32)
        window = jnp.roll(window, -shifts[layer_index, 1], axis=1)
        beside = jnp.roll(window, -1, axis=1)
        gains = layer_gains[layer_index]
        summed = summed + (
            gains[0] * window[:-1]
            + gains[1] * beside[:-1]
            + gains[2] * window[1:]
            + gains[3] * beside[1:]
        )
    return summed


def windows(array, axis, count, stride, width):
    parts = [
        lax.slice_in_dim(array, offset, offset + stride * (count - 1) + 1, stride=stride, axis=axis)
        for offset in range(width)
    ]
    return jnp.stack(parts, axis=axis + 1)


def on_device(screens, ray_shift, ray_weight, influence_index, influence, pupil_mask, petal):
    band_rows = screens.shape[1]
    rim_depth = SPAN * band_rows
    padded_rim = band_stack_whole(screens)
    phases = [
        trace_rows(padded_rim, ray_shift[member], ray_weight[member], rim_depth, band_rows)
        for member in range(ray_shift.shape[0])
    ]
    tile_count = lax.axis_size("tile")
    dir_count = lax.axis_size("dir")
    direction_count = ray_shift.shape[0] * dir_count
    summed = phases[0]
    for member in range(1, len(phases)):
        summed = summed + phases[member]
    mean_phase = (
        lax.psum_scatter(
            summed.astype(jnp.bfloat16), "dir", scatter_dimension=1, tiled=True
        ).astype(jnp.float32)
        / direction_count
    )
    tiles_here = influence.shape[1]
    near_count = influence.shape[2]
    block_rows, block_columns = petal.shape
    ext_rows, ext_columns = block_rows + 2, block_columns + 2
    extent = ext_rows * ext_columns
    values = influence.astype(jnp.float32)
    onehot = (influence_index[..., None] == jnp.arange(extent, dtype=jnp.int32)).astype(
        jnp.float32
    )
    weights = pupil_mask.astype(jnp.float32).reshape(band_rows, tiles_here, 128)

    masked = (influence * weights[:, :, None, :].astype(jnp.bfloat16))
    gram = jnp.einsum(
        "rckp,rcjp->rckj", masked, influence, preferred_element_type=jnp.float32
    )
    placed = jnp.einsum("rckj,rcjb->rckb", gram, onehot, precision=highest)
    block_matrix = jnp.einsum("rcka,rckb->ab", onehot, placed, precision=highest)

    field = (weights * mean_phase.reshape(band_rows, tiles_here, 128))
    tile_terms = jnp.einsum("rckp,rcp->rck", values, field, precision=highest)
    block_rhs = jnp.einsum("rck,rcka->a", tile_terms, onehot, precision=highest)

    payload = jnp.concatenate(
        [block_matrix.reshape(-1), block_rhs, petal.reshape(-1).astype(jnp.float32)]
    )
    gathered = lax.all_gather(payload, ("tile", "dir"), tiled=False)
    block_count = tile_count * dir_count
    matrices = gathered[:, : extent * extent].reshape(block_count, extent, extent)
    rhs_blocks = gathered[:, extent * extent : extent * extent + extent]
    petal_blocks = gathered[:, extent * extent + extent :].reshape(
        tile_count, dir_count, block_rows, block_columns
    )
    grid_rows, grid_columns = tile_count * block_rows, dir_count * block_columns
    petal_grid = petal_blocks.transpose(0, 2, 1, 3).reshape(grid_rows, grid_columns)
    active = (petal_grid < 6).astype(jnp.float32)
    petals = (petal_grid[:, :, None] == jnp.arange(6, dtype=jnp.float32)).astype(jnp.float32)

    def gather_blocks(padded):
        rows = windows(padded, 0, tile_count, block_rows, ext_rows)
        both = windows(rows, 2, dir_count, block_columns, ext_columns)
        return both.transpose(0, 2, 1, 3).reshape(block_count, extent)

    padded_shape = jax.ShapeDtypeStruct((grid_rows + 2, grid_columns + 2), jnp.float32)
    scatter_blocks = jax.linear_transpose(gather_blocks, padded_shape)

    def spread_blocks(blocks):
        (padded,) = scatter_blocks(blocks)
        return padded[1:-1, 1:-1]

    def operator(vector):
        picked = gather_blocks(jnp.pad(vector, 1))
        terms = jnp.einsum("bij,bj->bi", matrices, picked, precision=highest)
        local_part = active * spread_blocks(terms) + ridge_weight * vector
        petal_totals = jnp.einsum("ijp,ij->p", petals, vector, precision=highest)
        return local_part + piston_weight * jnp.einsum(
            "ijp,p->ij", petals, petal_totals, precision=highest
        )

    rhs = active * spread_blocks(rhs_blocks)
    commands = jnp.zeros_like(rhs)
    residual = rhs
    direction = rhs
    norm_now = jnp.sum(residual * residual)
    for step_index in range(ITERS):
        applied = operator(direction)
        step_size = norm_now / jnp.sum(direction * applied)
        commands = commands + step_size * direction
        residual = residual - step_size * applied
        norm_next = jnp.sum(residual * residual)
        direction = residual + (norm_next / norm_now) * direction
        norm_now = norm_next

    row_at = lax.axis_index("tile") * block_rows
    column_at = lax.axis_index("dir") * block_columns
    own = lax.dynamic_slice(commands, (row_at, column_at), (block_rows, block_columns))
    extended = lax.dynamic_slice(
        jnp.pad(commands, 1), (row_at, column_at), (ext_rows, ext_columns)
    )
    picked = jnp.einsum("rcka,a->rck", onehot, extended.reshape(-1), precision=highest)
    fitted = jnp.einsum("rckp,rck->rcp", values, picked, precision=highest).reshape(
        band_rows, tiles_here * 128
    )
    whole_band = lax.all_gather(fitted.astype(jnp.bfloat16), "dir", axis=1, tiled=True).astype(
        fitted.dtype
    )
    corrected = jnp.stack([(phase_rows - whole_band).astype(jnp.bfloat16) for phase_rows in phases])
    return (own, corrected)


def solution(mesh):
    in_specs = (
        P(None, "tile", None),
        P("dir", None, None),
        P("dir", None, None),
        P("tile", "dir", None),
        P("tile", "dir", None, None),
        P("tile", "dir"),
        P("tile", "dir"),
    )
    out_specs = (P("tile", "dir"), P("dir", "tile", None))
    return jax.shard_map(
        on_device, mesh=mesh, in_specs=in_specs, out_specs=out_specs, check_vma=False
    )
```

time: 734 us -> 497 us (0.68)
  blocking collectives: 221 us -> 14.3 us
  waiting for transfers between devices: 111 us -> 178 us
  starting transfers between devices: 65.3 us -> 6.3 us
  between operations: 96.2 us -> 68.7 us
  other arithmetic: 123 us -> 106 us
  local copies, waits for them, and re-layouts: 84.1 us -> 93.3 us
    psum x5 -> x0, blocking collectives: 207 us -> none  [the longest x3 124 us: on_device(): lax.psum((local_totals, jnp.sum(direction * local_part)), ('tile', 'dir'))]
    unnamed x1 -> x3, waiting for transfers between devices: 0.02 us -> 128 us
    ppermute x32 -> x0, starting transfers between devices: 59.5 us -> none  [the longest x16 38.6 us: padded_2(): before = lax.ppermute(last, axis, up)]
    ppermute x32 -> x0, waiting for transfers between devices: 56.2 us -> none  [the longest x16 56.1 us: padded_2(): after = lax.ppermute(first, axis, down)]
    pad x0 -> x59, local copies, waits for them, and re-layouts: none -> 20.5 us  [the longest x56 20.3 us: windows(): lax.slice_in_dim(array, offset, offset + stride * (count - 1) + 1, stride...]
    convert_element_type x1, other arithmetic: 96.7 us -> 86.4 us  [on_device(): summed.astype(jnp.bfloat16)]
    slice x52 -> x64, local copies, waits for them, and re-layouts: 37.7 us -> 30.2 us  [trace_rows(): beside = jnp.roll(window, -1, axis=1)]
    another operation x17 -> x56, local copies, waits for them, and re-layouts: 14.4 us -> 16.3 us  [windows(): return jnp.stack(parts, axis=axis + 1)]
  transfers between devices with their start and end apart: 37 -> 6, of which waited for: 19 -> 4; matrix products, arithmetic and copies ran while one was open for 3% -> 5% of each run, Pallas kernels for 0% -> 0%
where the time goes in v1:
time: 497 us; the launch traced here: 492 us
  waiting for transfers between devices  178 us (36%)
  other arithmetic  106 us (21%)
  local copies, waits for them, and re-layouts  93.3 us (19%)
  between operations  68.7 us (14%)
  matrix products  25.5 us (5%)
  blocking collectives  14.3 us (3%)
  starting transfers between devices  6.3 us (1%)
    unnamed x3, waiting for transfers between devices  128 us
    convert_element_type x1, other arithmetic, on_device(): summed.astype(jnp.bfloat16)  86.4 us
    ppermute x4, waiting for transfers between devices, passed_along(): lax.ppermute(array, axis, [(i, (i + by) % size) for i in range(size)])  37.1 us
    slice x64, local copies, waits for them, and re-layouts, trace_rows(): beside = jnp.roll(window, -1, axis=1)  30.2 us
    pad x56, local copies, waits for them, and re-layouts, windows(): lax.slice_in_dim(array, offset, offset + stride * (count - 1) + 1, stride...  20.3 us
    another operation x56, local copies, waits for them, and re-layouts, windows(): return jnp.stack(parts, axis=axis + 1)  16.3 us
    all_gather x1, blocking collectives, on_device(): lax.all_gather(fitted.astype(jnp.bfloat16), 'dir', axis=1, tiled=True)  14.3 us
    reduce_scatter x1, waiting for transfers between devices, on_device(): lax.psum_scatter(summed.astype(jnp.bfloat16), 'dir', scatter_dimension=1,...  12.4 us
  transfers between devices with their start and end apart: 6, of which 4 were waited for; matrix products, arithmetic and copies ran while one was open for 5% of the time, Pallas kernels for 0%

profile of v1, /device:TPU:0, one launch (start us, length us, event | category | flops | bytes accessed | tf_op | source)
XLA Modules:
  0.0 491.8 jit_solution(16747571693605617592)
XLA Ops:
  7.2 3.0 collective-permute-start
  10.2 2.6 collective-permute-start.2
  62.1 1.2 slice.1380
  68.2 1.4 iota_compare_fusion
  69.6 2.0 fusion.6
  71.6 1.5 constant_dynamic-update-slice_fusion.4
  73.1 5.6 %collective-permute-done.1 = bf16[6,64,2048]{2,1,0:T(8,128)(2,1)} collective-permute-done((bf16[6,64,2048]{2,1,0:T(8,128)(2,1)}, bf16[6,64,2048]{2,1,0:T(8,128)(2,1)}, u32[]{:S(2)}, u32[]{:S(2)}) %collective-permute-start.1) | collective-permute-done | bytes 1572896 | tf_op jit(solution)/shard_map/ppermute | solution.py:19
  78.8 1.5 constant_dynamic-update-slice_fusion.3
  80.5 1.5 constant_dynamic-update-slice_fusion.1
  82.0 31.5 %collective-permute-done.3 = bf16[6,64,2048]{2,1,0:T(8,128)(2,1)S(1)} collective-permute-done((bf16[6,64,2048]{2,1,0:T(8,128)(2,1)}, bf16[6,64,2048]{2,1,0:T(8,128)(2,1)S(1)}, u32[]{:S(2)}, u32[]{:S(2)}) %collective-permute-start.3) | collective-permute-done | bytes 1572896 | tf_op jit(solution)/shard_map/ppermute | solution.py:19
  113.6 1.3 fusion.226
  116.1 1.1 slice.1738
  117.5 1.0 slice.1745
  119.0 1.0 slice.1779
  120.4 1.1 slice.1815
  121.9 1.0 slice.1821
  123.3 1.0 slice.1851
  124.7 1.0 slice.1857
  126.2 1.0 slice.1785
  128.3 1.1 slice.1752
  131.2 1.1 slice.1791
  132.7 1.0 slice.1827
  134.1 1.0 slice.1833
  135.5 1.1 slice.1863
  137.0 1.0 slice.1869
  138.4 1.1 slice.1797
  140.6 1.1 slice.1766
  142.7 1.0 slice.1773
  144.8 1.0 slice.1803
  147.1 1.1 slice.1839
  149.1 1.1 slice.1845
  151.2 1.1 slice.1875
  153.3 1.0 slice.1881
  155.5 1.0 slice.1809
  157.4 86.4 %add_convert_fusion = (bf16[64,2048]{1,0:T(8,128)(2,1)}, f32[64,2048]{1,0:T(8,128)}, f32[64,2048]{1,0:T(8,128)}, f32[64,2048]{1,0:T(8,128)}, f32[64,2048]{1,0:T(8,128)}) fusion(f32[65,1]{1,0:T(8,128)} %slice.1810, f32[65,2047]{1,0:T(8,128)} %slice.1809, f32[]{:T(128)} %bitcast.99, f32[65,2048]{1,0:T(8,128)} %copy-done.28, f32[]{:T(128)} %bitcast.98, ...), kind=kLoop, calls=%fused_computation.386 | loop fusion | flops 31457280 | bytes 40305024 | tf_op jit(solution)/shard_map/convert_element_type | solution.py:74
  244.4 3.1 fusion.2
  247.5 3.7 fusion.8
  251.5 12.4 %reduce-scatter.2.cloned.1.call-done = bf16[64,512]{1,0:T(8,128)(2,1)} async-done(((bf16[64,2048]{1,0:T(8,128)(2,1)}), bf16[64,512]{1,0:T(8,128)(2,1)}) %reduce-scatter.2.cloned.1.call-update) | async-done | bytes 65552 | tf_op jit(solution)/shard_map/reduce_scatter | solution.py:73
  264.8 1.7 fusion.236
  266.6 1.0 fusion.11
  269.3 128.1 %all-reduce.83.cloned.1.call-done = f32[160192]{0:T(1024)} async-done(((f32[160192]{0:T(1024)}), f32[160192]{0:T(1024)}) %all-reduce.83.cloned.1.call-update) | async-done | bytes 640784
  397.4 1.4 reshape.525
  412.7 1.9 fusion.237
  432.8 1.9 fusion.238
  453.2 1.9 fusion.239
  464.6 2.8 fusion.4
  468.5 14.3 %all_gather.11 = bf16[64,2048]{1,0:T(8,128)(2,1)S(1)} all-gather(bf16[64,512]{1,0:T(8,128)(2,1)S(1)} %bitcast.579), channel_id=1, replica_groups=mesh['tile'=8,'dir'=4] {'dir'}, dimensions={1}, use_global_device_ids=true | all-gather | bytes 327680 | tf_op jit(solution)/shard_map/all_gather | solution.py:160
  483.6 1.1 pad_maximum_fusion
  (438 shorter events, 83.7 us)
Async XLA Ops:
  7.2 57.4 %copy-start.39 = (f32[4,6,4]{1,2,0:T(4,128)S(1)}, f32[4,6,4]{1,2,0:T(4,128)}, u32[]{:S(2)}) copy-start(f32[4,6,4]{1,2,0:T(4,128)} %param.11) | copy-start | bytes 1156
  7.2 61.0 %copy-start.40 = (s32[64,4,16]{0,2,1:T(8,128)S(1)}, s32[64,4,16]{0,2,1:T(8,128)}, u32[]{:S(2)}) copy-start(s32[64,4,16]{0,2,1:T(8,128)} %param.12) | copy-start | bytes 49156
  7.2 62.4 %copy-start.29 = (bf16[64,4,16,128]{3,2,1,0:T(8,128)(2,1)S(1)}, bf16[64,4,16,128]{3,2,1,0:T(8,128)(2,1)}, u32[]{:S(2)}) copy-start(bf16[64,4,16,128]{3,2,1,0:T(8,128)(2,1)} %param.13) | copy-start | bytes 3145732
  7.2 256.7 %reduce-scatter.2.cloned.1.call-start = ((), (), s32[]{:S(2)}) async-start(), calls=%async_computation.1 | async-start | bytes 327680 | tf_op jit(solution)/shard_map/reduce_scatter | solution.py:73
  7.2 64.4 %collective-permute-start = (bf16[6,64,2048]{2,1,0:T(8,128)(2,1)}, bf16[6,64,2048]{2,1,0:T(8,128)(2,1)}, u32[]{:S(2)}, u32[]{:S(2)}) collective-permute-start(bf16[6,64,2048]{2,1,0:T(8,128)(2,1)} %param.9), channel_id=1, source_target_pairs={{0,8},{4,12},{8,16},{12,20},{16,24},{20,28},{24,0},{28,4},{1,9},{5... | collective-permute-start | bytes 4718600 | tf_op jit(solution)/shard_map/ppermute | solution.py:19
  10.2 68.5 %collective-permute-start.1 = (bf16[6,64,2048]{2,1,0:T(8,128)(2,1)}, bf16[6,64,2048]{2,1,0:T(8,128)(2,1)}, u32[]{:S(2)}, u32[]{:S(2)}) collective-permute-start(bf16[6,64,2048]{2,1,0:T(8,128)(2,1)} %param.9), channel_id=1, source_target_pairs={{0,4},{4,8},{8,12},{12,16},{16,20},{20,24},{24,28},{28,0},{1,5},{5... | collective-permute-start | bytes 4718600 | tf_op jit(solution)/shard_map/ppermute | solution.py:19
  10.2 70.2 %collective-permute-start.2 = (bf16[6,64,2048]{2,1,0:T(8,128)(2,1)}, bf16[6,64,2048]{2,1,0:T(8,128)(2,1)}, u32[]{:S(2)}, u32[]{:S(2)}) collective-permute-start(bf16[6,64,2048]{2,1,0:T(8,128)(2,1)} %param.9), channel_id=1, source_target_pairs={{0,28},{4,0},{8,4},{12,8},{16,12},{20,16},{24,20},{28,24},{1,29},{... | collective-permute-start | bytes 4718600 | tf_op jit(solution)/shard_map/ppermute | solution.py:19
  12.9 100.6 %collective-permute-start.3 = (bf16[6,64,2048]{2,1,0:T(8,128)(2,1)}, bf16[6,64,2048]{2,1,0:T(8,128)(2,1)S(1)}, u32[]{:S(2)}, u32[]{:S(2)}) collective-permute-start(bf16[6,64,2048]{2,1,0:T(8,128)(2,1)} %param.9), channel_id=1, source_target_pairs={{0,24},{4,28},{8,0},{12,4},{16,8},{20,12},{24,16},{28,20},{1,25},{... | collective-permute-start | bytes 4718600 | tf_op jit(solution)/shard_map/ppermute | solution.py:19
  73.1 7.2 %copy-start.37 = (bf16[6,64,2048]{2,1,0:T(8,128)(2,1)S(1)}, bf16[6,64,2048]{2,1,0:T(8,128)(2,1)}, u32[]{:S(2)}) copy-start(bf16[6,64,2048]{2,1,0:T(8,128)(2,1)} %param.9) | copy-start | bytes 4718596
  116.1 2.5 copy-start
  117.5 2.5 copy-start.2
  119.0 2.5 copy-start.4
  120.4 2.5 copy-start.6
  121.9 2.5 copy-start.8
  123.3 2.5 copy-start.10
  124.7 2.5 copy-start.11
  128.3 2.5 copy-start.13
  129.8 2.5 copy-start.14
  131.2 2.5 copy-start.15
  132.6 2.5 copy-start.16
  134.1 2.5 copy-start.17
  135.5 2.5 copy-start.18
  137.0 2.5 copy-start.19
  140.6 3.1 copy-start.21
  142.7 3.1 copy-start.22
  144.8 3.4 copy-start.23
  147.1 3.1 copy-start.24
  149.1 3.1 copy-start.25
  151.2 3.2 copy-start.26
  153.3 3.3 copy-start.27
  153.3 3.9 copy-start.9
  153.3 3.9 slice-start.12
  153.3 3.9 slice-start.13
  153.3 3.9 slice-start.14
  153.3 3.9 slice-start.15
  155.0 2.3 copy-start.5
  155.0 2.3 slice-start.2
  243.9 3.6 copy-start.41
  243.9 153.6 %all-reduce.83.cloned.1.call-start = ((), (), s32[]{:S(2)}) async-start(), calls=%async_computation.2 | async-start | bytes 1286144
  247.5 3.9 copy-start.42
  247.5 16.4 %copy-start.38 = (s32[64,512]{1,0:T(8,128)S(1)}, s32[64,512]{1,0:T(8,128)}, u32[]{:S(2)}) copy-start(s32[64,512]{1,0:T(8,128)} %param.14) | copy-start | bytes 393220
  247.5 17.3 %copy-start.30 = (bf16[64,4,16,128]{3,2,1,0:T(8,128)(2,1)S(1)}, bf16[64,4,16,128]{3,2,1,0:T(8,128)(2,1)}, u32[]{:S(2)}) copy-start(bf16[64,4,16,128]{3,2,1,0:T(8,128)(2,1)} %param.13) | copy-start | bytes 3145732
  398.9 7.7 %copy-start.31 = (f32[32,5006]{1,0:T(8,128)}, f32[32,5006]{1,0:T(8,128)S(1)}, u32[]{:S(2)}) copy-start(f32[32,5006]{1,0:T(8,128)S(1)} %reshape.525) | copy-start | bytes 1922308
  408.0 4.1 slice-start.16
  467.3 16.1 %copy-start.33 = (f32[64,2048]{1,0:T(8,128)S(1)}, f32[64,2048]{1,0:T(8,128)}, u32[]{:S(2)}) copy-start(f32[64,2048]{1,0:T(8,128)} %get-tuple-element.13) | copy-start | bytes 1572868
  467.3 16.1 %copy-start.34 = (f32[64,2048]{1,0:T(8,128)S(1)}, f32[64,2048]{1,0:T(8,128)}, u32[]{:S(2)}) copy-start(f32[64,2048]{1,0:T(8,128)} %get-tuple-element.14) | copy-start | bytes 1572868
  467.3 16.1 %copy-start.35 = (f32[64,2048]{1,0:T(8,128)S(1)}, f32[64,2048]{1,0:T(8,128)}, u32[]{:S(2)}) copy-start(f32[64,2048]{1,0:T(8,128)} %get-tuple-element.15) | copy-start | bytes 1572868
  467.3 16.1 %copy-start.36 = (f32[64,2048]{1,0:T(8,128)S(1)}, f32[64,2048]{1,0:T(8,128)}, u32[]{:S(2)}) copy-start(f32[64,2048]{1,0:T(8,128)} %get-tuple-element.16) | copy-start | bytes 1572868
  (18 other events, 36.1 us)
Sparse Core Ops, SparseCore 0:
  244.0 19.8 reduce-scatter.1
  270.5 126.8 all-reduce.82
